TPU v7x, 256 devices: a whole 4x4x8 slice. The times are simulated.
256 devices in a mesh: dp: 64 (over z, x, core), mp: 4 (over y).
Axes of the slice: x: 4, y: 4, z: 8, core: 2. Of those that a mesh axis runs over, the one named last changes fastest.
Arguments:
- embed_table: float32 [16, 32768, 256], P('mp', 'dp'), may hold values from -5 to 5
- accum: float32 [16, 32768], P('mp', 'dp'), may hold values from 0.1 to 3
- stale_grad: bfloat16 [16, 32768, 256], P('mp', 'dp'), may hold values from -6 to 6
- grad_owner: int32 [16, 32768, 1], P('mp', 'dp'), may hold values from 0 to 63; in each aligned block of 512 rows (0 to 511, 512 to 1023, ..., all dimensions but the last counted through in order) at most 16 rows name the same one
- grad_row: int32 [16, 32768], P('mp', 'dp'), may hold values from 0 to 511
- lookup_owner: int32 [16, 32768, 1], P('mp', 'dp'), may hold values from 0 to 63; in each aligned block of 512 rows (0 to 511, 512 to 1023, ..., all dimensions but the last counted through in order) at most 16 rows name the same one
- lookup_row: int32 [16, 32768], P('mp', 'dp'), may hold values from 0 to 511
- bag_len: int32 [16, 16384], P('mp', 'dp'), may hold values from 1 to 2
- label: int32 [16384], P('dp'), may hold values 0 or 1
- up_factor_weight: bfloat16 [2, 512, 4096], P(None, None, 'mp'), may hold values from -0.25 to 0.25
- v_weight: bfloat16 [2, 512, 4096], P(None, None, 'mp'), may hold values from -0.09375 to 0.09375
- cross_bias: float32 [2, 4096], P(None, 'mp'), may hold values from -3 to 3
- head_weight: float32 [4096], P('mp'), may hold values from -0.09375 to 0.09375
Outputs:
- new_table: float32 [16, 32768, 256], P('mp', 'dp')
- new_accum: float32 [16, 32768], P('mp', 'dp')
- grad_u: float32 [2, 512, 4096], P(None, 'dp', 'mp')
- grad_v: float32 [2, 512, 4096], P(None, 'dp', 'mp')
- grad_small: float32 [3, 4096], P(None, 'mp')
- grad_pooled: bfloat16 [16384, 4096], P('dp', 'mp')
Inputs may be any that keep to these rules, and one draw needn't show every extreme that they name: `grad_owner`: among the 512 blocks of one feature held by one index of dp, at most 16 name the same owner, and in some such group exactly 16 do. `lookup_owner`: among the 512 id slots of one feature belonging to one index of dp, at most 16 name the same owner, and in some such group exactly 16 do; slots k >= bag_len are unused.
All inputs are finite; a program needn't handle non-finite values. No bound on the sum of `label` on one device may be relied on, other than what follows from the above.
Results may differ from a plain program's by a relative error of at most 0.009.
Values may be sent and summed in bfloat16 or wider, within the bound.
No kernel may reach another device: no remote copies, remote signals or barrier semaphores. Data moves between devices by JAX's collectives and lax.ppermute only.
A program may use at most 128 MiB of HBM per device.

v0:
```python
import jax
import jax.numpy as jnp
from jax import lax
from jax.sharding import PartitionSpec as P

learn_rate = 0.5


def in_blocks(array, dim, devices):
    shape = array.shape
    parts = array.reshape(*shape[:dim], devices, shape[dim] // devices, *shape[dim + 1 :])
    return jnp.moveaxis(parts, dim, 0)


def sum_at_owner(array, axis, dim):
    parts = in_blocks(array, dim, lax.axis_size(axis))
    arrived = lax.all_to_all(parts, axis, split_axis=0, concat_axis=0, tiled=True)
    return arrived.sum(axis=0)


def copy_for_each(array, axis):
    copies = jnp.broadcast_to(array, (lax.axis_size(axis), *array.shape))
    return lax.all_to_all(copies, axis, split_axis=0, concat_axis=0, tiled=True)


def over_copies(array, axis):
    return copy_for_each(array, axis).sum(axis=0)


def side_by_side(arrays, axis, dim, along):
    widths = [a.shape[along] for a in arrays]
    both = jnp.concatenate(arrays, axis=along)
    filled = lax.psum_scatter(both, axis, scatter_dimension=dim, tiled=True)
    return tuple(jnp.split(filled, [sum(widths[:k]) for k in range(1, len(widths))], axis=along))


def bucket_slots(owners, capacity, peers):
    count = owners.shape[1]
    onehot = (owners[:, None, :] == jnp.arange(peers)[None, :, None]).astype(jnp.bfloat16)
    earlier = (jnp.arange(count)[:, None] < jnp.arange(count)[None, :]).astype(jnp.bfloat16)
    before = jnp.einsum("fpi,ij->fpj", onehot, earlier, preferred_element_type=jnp.float32)
    order_in = jnp.sum(before * onehot.astype(jnp.float32), axis=1)
    return owners * capacity + order_in.astype(jnp.int32)


def selection_matrix(indices, length):
    return (indices[:, :, None] == jnp.arange(length)[None, None, :]).astype(jnp.bfloat16)


def contract_last(left, right):
    return lax.dot_general(
        left, right, (((1,), (1,)), ((), ())), preferred_element_type=jnp.float32
    )


def contract_first(left, right):
    return lax.dot_general(
        left, right, (((0,), (0,)), ((), ())), preferred_element_type=jnp.float32
    )


def summed_rounded(partial, axis):
    share = lax.psum_scatter(partial, axis, scatter_dimension=0, tiled=True)
    return lax.all_gather(share.astype(jnp.bfloat16), axis, axis=0, tiled=True)


def cross_down(state, v_layer):
    return summed_rounded(contract_last(state, v_layer), "mp")


def local(
    embed_table,
    accum,
    stale_grad,
    grad_owner,
    grad_row,
    lookup_owner,
    lookup_row,
    bag_len,
    label,
    up_factor_weight,
    v_weight,
    cross_bias,
    head_weight,
):
    peers = lax.axis_size("dp")
    local_feats, grad_dev, width = stale_grad.shape
    rows_per_shard = embed_table.shape[1]
    which_feature = jnp.arange(local_feats)[:, None]
    grad_cap = max(2, 2 * grad_dev // peers)
    grad_total = peers * grad_cap
    grad_slot = bucket_slots(grad_owner[:, :, 0], grad_cap, peers)
    place = selection_matrix(grad_slot, grad_total)
    send_grads = jnp.einsum(
        "fns,fne->fse", place, stale_grad, preferred_element_type=jnp.float32
    ).astype(jnp.bfloat16)
    send_rows = (
        jnp.full((local_feats, grad_total), rows_per_shard, jnp.int32)
        .at[which_feature, grad_slot]
        .set(grad_row)
    )
    recv_grads = lax.all_to_all(
        send_grads.reshape(local_feats, peers, grad_cap, width),
        "dp",
        split_axis=1,
        concat_axis=1,
        tiled=True,
    )
    recv_rows = lax.all_to_all(
        send_rows.reshape(local_feats, peers, grad_cap),
        "dp",
        split_axis=1,
        concat_axis=1,
        tiled=True,
    )
    landing = selection_matrix(recv_rows.reshape(local_feats, grad_total), rows_per_shard)
    summed = jnp.einsum(
        "wjc,wjl->wcl",
        landing,
        recv_grads.reshape(local_feats, grad_total, width),
        preferred_element_type=jnp.float32,
    )
    new_accum = accum + jnp.mean(summed * summed, axis=2)
    new_table = embed_table - learn_rate * summed / jnp.sqrt(new_accum)[:, :, None]
    batch_dev = bag_len.shape[1]
    look_dev = lookup_row.shape[1]
    bag_size = look_dev // batch_dev
    look_cap = max(2, 2 * look_dev // peers)
    look_total = peers * look_cap
    look_slot = bucket_slots(lookup_owner[:, :, 0], look_cap, peers)
    wanted = (
        jnp.zeros((local_feats, look_total), jnp.int32).at[which_feature, look_slot].set(lookup_row)
    )
    requested_ids = lax.all_to_all(
        wanted.reshape(local_feats, peers, look_cap), "dp", split_axis=1, concat_axis=1, tiled=True
    ).reshape(local_feats, look_total)
    second_table = embed_table.astype(jnp.bfloat16)
    served = jnp.einsum(
        "adv,avm->adm",
        selection_matrix(requested_ids, rows_per_shard),
        second_table,
        preferred_element_type=jnp.float32,
    ).astype(jnp.bfloat16)
    returned = lax.all_to_all(
        served.reshape(local_feats, peers, look_cap, width),
        "dp",
        split_axis=1,
        concat_axis=1,
        tiled=True,
    ).reshape(local_feats, look_total, width)
    slots = look_slot.reshape(local_feats, batch_dev, bag_size)
    mixing = jnp.zeros((local_feats, batch_dev, look_total), jnp.bfloat16)
    for member in range(bag_size):
        used = (bag_len > member).astype(jnp.bfloat16)
        mixing = mixing + selection_matrix(slots[:, :, member], look_total) * used[:, :, None]
    pooled = jnp.einsum(
        "fbs,fse->fbe", mixing, returned, preferred_element_type=jnp.float32
    ).astype(jnp.bfloat16)
    start = jnp.transpose(pooled, (1, 0, 2)).reshape(batch_dev, local_feats * width)
    start_f = start.astype(jnp.float32)
    n_layers = up_factor_weight.shape[0]
    state = start
    states = []
    downs = []
    crosses = []
    for layer in range(n_layers):
        down_sum = cross_down(state, v_weight[layer])
        cross_out = (
            jnp.dot(down_sum, up_factor_weight[layer], preferred_element_type=jnp.float32)
            + cross_bias[layer]
        )
        states.append(state)
        downs.append(down_sum)
        crosses.append(cross_out)
        state = (start_f * cross_out + state.astype(jnp.float32)).astype(jnp.bfloat16)
    logit = lax.psum(jnp.sum(state.astype(jnp.float32) * head_weight[None, :], axis=1), "mp")
    slope = (jax.nn.sigmoid(logit) - label.astype(jnp.float32)) / jnp.sqrt(
        jnp.float32(batch_dev * peers)
    )
    upstream = slope[:, None] * head_weight[None, :]
    head_grad = jnp.sum(slope[:, None] * state.astype(jnp.float32), axis=0)
    to_start = jnp.zeros(start_f.shape, jnp.float32)
    grads_u = [None] * n_layers
    grads_v = [None] * n_layers
    bias_grads = [None] * n_layers
    for layer in reversed(range(n_layers)):
        direct = upstream * start_f
        bias_grads[layer] = jnp.sum(direct, axis=0)
        direct_bias_term = direct.astype(jnp.bfloat16)
        grad_u_layer = contract_first(downs[layer], direct_bias_term)
        back_sum = summed_rounded(contract_last(direct_bias_term, up_factor_weight[layer]), "mp")
        down_factor_gradient = contract_first(back_sum, states[layer])
        to_start = to_start + upstream * crosses[layer]
        upstream = upstream + jnp.dot(back_sum, v_weight[layer], preferred_element_type=jnp.float32)
        grads_u[layer] = grad_u_layer
        grads_v[layer] = down_factor_gradient
    grad_u = jnp.stack(grads_u)
    grad_v = jnp.stack(grads_v)
    grad_u, grad_v = side_by_side((grad_u, grad_v), "dp", 1, 0)
    grad_small = lax.psum(jnp.stack(bias_grads + [head_grad]), "dp")
    grad_pooled = (upstream + to_start).astype(jnp.bfloat16)
    return (new_table, new_accum, grad_u, grad_v, grad_small, grad_pooled)


def solution(mesh):
    return jax.shard_map(
        local,
        mesh=mesh,
        in_specs=(
            P("mp", "dp", None),
            P("mp", "dp"),
            P("mp", "dp", None),
            P("mp", "dp", None),
            P("mp", "dp"),
            P("mp", "dp", None),
            P("mp", "dp"),
            P("mp", "dp"),
            P("dp"),
            P(None, None, "mp"),
            P(None, None, "mp"),
            P(None, "mp"),
            P("mp"),
        ),
        out_specs=(
            P("mp", "dp", None),
            P("mp", "dp"),
            P(None, "dp", "mp"),
            P(None, "dp", "mp"),
            P(None, "mp"),
            P("dp", "mp"),
        ),
        check_vma=False,
    )
```

profile of v0, /device:TPU:0, one launch (start us, length us, event | category | flops | bytes accessed | tf_op | source)
XLA Modules:
  0.0 633.7 jit_solution(6955148603846393421)
XLA Ops:
  10.6 8.1 %scatter_custom_fusion.1 = s32[4096]{0:T(1024)S(1)} fusion(s32[2048]{0:T(1024)S(1)} %bitcast.111, s32[2048]{0:T(1024)S(1)} %bitcast.113, s32[]{:T(128)} %constant.5.clone.1), kind=kCustom, calls=%fused_computation.105 | custom fusion | bytes 16388
  18.9 21.1 %all_to_all.20 = s32[4,64,16]{2,0,1:T(4,128)S(1)} all-to-all(s32[4,64,16]{2,0,1:T(4,128)S(1)} %copy.43), channel_id=1, replica_groups=mesh['dp'=64,'mp'=4] {'dp'}, dimensions={1} | all-to-all | bytes 32768 | tf_op jit(solution)/shard_map/all_to_all | solution.py:134
  43.8 4.7 all-to-all-start.3
  51.0 48.8 %all-to-all-done.3 = bf16[4,64,16,256]{3,2,0,1:T(8,128)(2,1)S(1)} async-done(((bf16[4,64,16,256]{3,2,0,1:T(8,128)(2,1)}), bf16[4,64,16,256]{3,2,0,1:T(8,128)(2,1)S(1)}, u32[]{:S(2)}, u32[]{:S(2)}) %all-to-all-start.3) | async-done | bytes 2097184 | tf_op jit(solution)/shard_map/all_to_all | solution.py:144
  103.7 20.2 %reduce-scatter.6.cloned.1.call-done = f32[64,512]{1,0:T(8,128)} async-done(((f32[256,512]{1,0:T(8,128)}), f32[64,512]{1,0:T(8,128)}) %reduce-scatter.6.cloned.1.call-update) | async-done | bytes 131088 | tf_op jit(solution)/shard_map/reduce_scatter | solution.py:63
  125.0 12.3 %all_gather.12 = bf16[256,512]{1,0:T(8,128)(2,1)S(1)} all-gather(bf16[64,512]{1,0:T(8,128)(2,1)S(1)} %convert_element_type.138), channel_id=1, replica_groups=mesh['dp'=64,'mp'=4] {'mp'}, dimensions={0}, use_global_device_ids=true | all-gather | bytes 327680 | tf_op jit(solution)/shard_map/all_gather | solution.py:64
  141.5 23.9 %reduce-scatter.8.cloned.1.call-done = f32[64,512]{1,0:T(8,128)} async-done(((f32[256,512]{1,0:T(8,128)}), f32[64,512]{1,0:T(8,128)}) %reduce-scatter.8.cloned.1.call-update) | async-done | bytes 131088 | tf_op jit(solution)/shard_map/reduce_scatter | solution.py:63
  166.3 12.3 %all_gather.13 = bf16[256,512]{1,0:T(8,128)(2,1)S(1)} all-gather(bf16[64,512]{1,0:T(8,128)(2,1)S(1)} %convert_element_type.141), channel_id=1, replica_groups=mesh['dp'=64,'mp'=4] {'mp'}, dimensions={0}, use_global_device_ids=true | all-gather | bytes 327680 | tf_op jit(solution)/shard_map/all_gather | solution.py:64
  178.5 2.9 fusion.23
  181.4 8.4 %psum.14 = f32[256]{0:T(256)S(1)} all-reduce(f32[256]{0:T(256)S(1)} %get-tuple-element.28), channel_id=1, replica_groups=mesh['dp'=64,'mp'=4] {'mp'}, use_global_device_ids=true, to_apply=%region_8.0 | all-reduce | flops 256 | bytes 2048 | tf_op jit(solution)/shard_map/psum | solution.py:176
  192.8 23.7 %reduce-scatter.10.cloned.1.call-done = f32[64,512]{1,0:T(8,128)} async-done(((f32[256,512]{1,0:T(8,128)}), f32[64,512]{1,0:T(8,128)}) %reduce-scatter.10.cloned.1.call-update) | async-done | bytes 131088 | tf_op jit(solution)/shard_map/reduce_scatter | solution.py:63
  217.5 12.3 %all_gather.14 = bf16[256,512]{1,0:T(8,128)(2,1)S(1)} all-gather(bf16[64,512]{1,0:T(8,128)(2,1)S(1)} %convert_element_type.149), channel_id=1, replica_groups=mesh['dp'=64,'mp'=4] {'mp'}, dimensions={0}, use_global_device_ids=true | all-gather | bytes 327680 | tf_op jit(solution)/shard_map/all_gather | solution.py:64
  239.3 18.1 %reduce-scatter.12.cloned.1.call-done = f32[64,512]{1,0:T(8,128)} async-done(((f32[256,512]{1,0:T(8,128)}), f32[64,512]{1,0:T(8,128)}) %reduce-scatter.12.cloned.1.call-update) | async-done | bytes 131088 | tf_op jit(solution)/shard_map/reduce_scatter | solution.py:63
  258.5 12.3 %all_gather.15 = bf16[256,512]{1,0:T(8,128)(2,1)S(1)} all-gather(bf16[64,512]{1,0:T(8,128)(2,1)S(1)} %convert_element_type.152), channel_id=1, replica_groups=mesh['dp'=64,'mp'=4] {'mp'}, dimensions={0}, use_global_device_ids=true | all-gather | bytes 327680 | tf_op jit(solution)/shard_map/all_gather | solution.py:64
  271.2 5.2 pad_maximum_fusion
  277.1 8.1 %scatter_custom_fusion = s32[4096]{0:T(1024)S(1)} fusion(s32[2048]{0:T(1024)S(1)} %bitcast.112, s32[2048]{0:T(1024)S(1)} %bitcast.114, s32[]{:T(128)} %constant.11.clone.1), kind=kCustom, calls=%fused_computation.107 | custom fusion | bytes 16388
  286.0 10.4 %all-to-all-start = ((s32[4,64,16]{2,0,1:T(4,128)}), s32[4,64,16]{2,0,1:T(4,128)S(1)}, u32[]{:S(2)}, u32[]{:S(2)}) async-start(s32[4,64,16]{2,0,1:T(4,128)} %copy.33), calls=%async_computation | async-start | bytes 262144 | tf_op jit(solution)/shard_map/all_to_all | solution.py:109
  299.6 7.9 %all-to-all-done = s32[4,64,16]{2,0,1:T(4,128)S(1)} async-done(((s32[4,64,16]{2,0,1:T(4,128)}), s32[4,64,16]{2,0,1:T(4,128)S(1)}, u32[]{:S(2)}, u32[]{:S(2)}) %all-to-all-start) | async-done | bytes 16416 | tf_op jit(solution)/shard_map/all_to_all | solution.py:109
  307.5 5.6 all-to-all-start.1
  313.1 2.9 copy.38
  316.2 49.0 %all-to-all-done.1 = bf16[4,64,16,256]{3,2,0,1:T(8,128)(2,1)} async-done(((bf16[4,64,16,256]{3,2,0,1:T(8,128)(2,1)}), bf16[4,64,16,256]{3,2,0,1:T(8,128)(2,1)}, u32[]{:S(2)}, u32[]{:S(2)}) %all-to-all-start.1) | async-done | bytes 2097184 | tf_op jit(solution)/shard_map/all_to_all | solution.py:102
  367.0 2.9 multiply_reduce_fusion
  372.4 3.0 copy.49
  376.6 246.2 %psum.15 = f32[3,1024]{1,0:T(4,128)} all-reduce(f32[3,1024]{1,0:T(4,128)S(1)} %pad_maximum_fusion.1), channel_id=1, replica_groups=mesh['dp'=64,'mp'=4] {'dp'}, use_global_device_ids=true, to_apply=%region_15.0 | all-reduce | flops 3072 | bytes 24576 | tf_op jit(solution)/shard_map/psum | solution.py:200
  (124 shorter events, 49.4 us)
Async XLA Ops:
  7.2 289.3 %copy-start = (bf16[4,512,256]{2,1,0:T(8,128)(2,1)S(1)}, bf16[4,512,256]{2,1,0:T(8,128)(2,1)}, u32[]{:S(2)}) copy-start(bf16[4,512,256]{2,1,0:T(8,128)(2,1)} %param.15) | copy-start | bytes 3145732
  7.2 3.1 copy-start.23
  7.2 3.2 copy-start.22
  7.2 3.0 copy-start.15
  7.2 3.4 copy-start.16
  7.2 32.8 %copy-start.9 = (f32[4,512,256]{2,1,0:T(8,128)S(1)}, f32[4,512,256]{2,1,0:T(8,128)}, u32[]{:S(2)}) copy-start(f32[4,512,256]{2,1,0:T(8,128)} %param.13) | copy-start | bytes 6291460
  43.8 56.1 %all-to-all-start.3 = ((bf16[4,64,16,256]{3,2,0,1:T(8,128)(2,1)}), bf16[4,64,16,256]{3,2,0,1:T(8,128)(2,1)S(1)}, u32[]{:S(2)}, u32[]{:S(2)}) async-start(bf16[4,64,16,256]{3,2,0,1:T(8,128)(2,1)} %copy.45), calls=%async_computation.3 | async-start | bytes 4194304 | tf_op jit(solution)/shard_map/all_to_all | solution.py:144
  48.5 2.5 copy-start.20
  48.5 75.4 %reduce-scatter.6.cloned.1.call-start = ((), (), s32[]{:S(2)}) async-start(), calls=%async_computation.9 | async-start | bytes 655360 | tf_op jit(solution)/shard_map/reduce_scatter | solution.py:63
  103.4 61.9 %reduce-scatter.8.cloned.1.call-start = ((), (), s32[]{:S(2)}) async-start(), calls=%async_computation.10 | async-start | bytes 655360 | tf_op jit(solution)/shard_map/reduce_scatter | solution.py:63
  123.9 16.2 %copy-start.13 = (bf16[2,512,1024]{2,1,0:T(8,128)(2,1)S(1)}, bf16[2,512,1024]{2,1,0:T(8,128)(2,1)}, u32[]{:S(2)}) copy-start(bf16[2,512,1024]{2,1,0:T(8,128)(2,1)} %param.23) | copy-start | bytes 6291460
  137.3 4.1 copy-start.7
  140.1 41.3 %copy-start.4 = (bf16[256,1024]{1,0:T(8,128)(2,1)}, bf16[256,1024]{1,0:T(8,128)(2,1)S(1)}, u32[]{:S(2)}) copy-start(bf16[256,1024]{1,0:T(8,128)(2,1)S(1)} %get-tuple-element.48) | copy-start | bytes 1572868
  141.4 75.1 %reduce-scatter.10.cloned.1.call-start = ((), (), s32[]{:S(2)}) async-start(), calls=%async_computation.11 | async-start | bytes 655360 | tf_op jit(solution)/shard_map/reduce_scatter | solution.py:63
  166.2 23.5 %copy-start.21 = (s32[256]{0:T(256)S(1)}, s32[256]{0:T(256)}, u32[]{:S(2)}) copy-start(s32[256]{0:T(256)} %param.21) | copy-start | bytes 3076
  192.7 64.7 %reduce-scatter.12.cloned.1.call-start = ((), (), s32[]{:S(2)}) async-start(), calls=%async_computation.12 | async-start | bytes 655360 | tf_op jit(solution)/shard_map/reduce_scatter | solution.py:63
  216.5 15.7 %copy-start.3 = (bf16[2,512,1024]{2,1,0:T(8,128)(2,1)S(1)}, bf16[2,512,1024]{2,1,0:T(8,128)(2,1)}, u32[]{:S(2)}) copy-start(bf16[2,512,1024]{2,1,0:T(8,128)(2,1)} %param.22) | copy-start | bytes 6291460
  233.5 392.1 %reduce-scatter.14.cloned.1.call-start = ((), (), s32[]{:S(2)}) async-start(), calls=%async_computation.13 | async-start | bytes 8519680 | tf_op jit(solution)/shard_map/reduce_scatter | solution.py:33
  257.4 13.8 %copy-start.2 = (f32[1,512,1024]{2,1,0:T(8,128)S(1)}, f32[1,512,1024]{2,1,0:T(8,128)}, u32[]{:S(2)}) copy-start(f32[1,512,1024]{2,1,0:T(8,128)} %convolution_bitcast_fusion.2) | copy-start | bytes 6291460
  286.0 21.5 %all-to-all-start = ((s32[4,64,16]{2,0,1:T(4,128)}), s32[4,64,16]{2,0,1:T(4,128)S(1)}, u32[]{:S(2)}, u32[]{:S(2)}) async-start(s32[4,64,16]{2,0,1:T(4,128)} %copy.33), calls=%async_computation | async-start | bytes 262144 | tf_op jit(solution)/shard_map/all_to_all | solution.py:109
  307.5 57.6 %all-to-all-start.1 = ((bf16[4,64,16,256]{3,2,0,1:T(8,128)(2,1)}), bf16[4,64,16,256]{3,2,0,1:T(8,128)(2,1)}, u32[]{:S(2)}, u32[]{:S(2)}) async-start(bf16[4,64,16,256]{3,2,0,1:T(8,128)(2,1)} %copy.35), calls=%async_computation.1 | async-start | bytes 4194304 | tf_op jit(solution)/shard_map/all_to_all | solution.py:102
  366.9 2.9 copy-start.19
  367.0 3.5 copy-start.1
  372.4 250.5 %copy-start.6 = (f32[256,1024]{1,0:T(8,128)S(1)}, f32[256,1024]{1,0:T(8,128)}, u32[]{:S(2)}) copy-start(f32[256,1024]{1,0:T(8,128)} %get-tuple-element.50) | copy-start | bytes 3145732
  (8 other events, 11.8 us)
Sparse Core Ops, SparseCore 0:
  103.5 20.3 reduce-scatter.5
  141.5 23.7 reduce-scatter.7
  192.8 23.5 reduce-scatter.9
  233.7 23.7 reduce-scatter.11
  276.6 150.7 reduce-scatter.13
where the time goes:
time: 635 us; the launch traced here: 634 us
  blocking collectives  325 us (51%)
  waiting for transfers between devices  192 us (30%)
  local copies, waits for them, and re-layouts  34.7 us (5%)
  matrix products  31.7 us (5%)
  starting transfers between devices  21.1 us (3%)
  other arithmetic  15.5 us (2%)
  between operations  14.3 us (2%)
    psum x1, blocking collectives, local(): grad_small = lax.psum(jnp.stack(bias_grads + [head_grad]), 'dp')  246 us
    reduce_scatter x4, waiting for transfers between devices, summed_rounded(): share = lax.psum_scatter(partial, axis, scatter_dimension=0, tiled=True)  85.9 us
    all_gather x4, blocking collectives, summed_rounded(): return lax.all_gather(share.astype(jnp.bfloat16), axis, axis=0, tiled=True)  49 us
    all_to_all x1, waiting for transfers between devices, local(): lax.all_to_all(send_grads.reshape(local_feats, peers, grad_cap, width), '...  49 us
    all_to_all x1, waiting for transfers between devices, local(): lax.all_to_all(served.reshape(local_feats, peers, look_cap, width), 'dp',...  48.8 us
    unnamed x60, local copies, waits for them, and re-layouts  25.1 us
    all_to_all x1, blocking collectives, local(): lax.all_to_all(wanted.reshape(local_feats, peers, look_cap), 'dp', split_...  21.1 us
  transfers between devices with their start and end apart: 8, of which 7 were waited for; matrix products, arithmetic and copies ran while one was open for 6% of the time, Pallas kernels for 0%

commit v1 on v0

--- a/solution.py
+++ b/solution.py
@@ -106,13 +106,12 @@
         concat_axis=1,
         tiled=True,
     )
-    recv_rows = lax.all_to_all(
-        send_rows.reshape(local_feats, peers, grad_cap),
-        "dp",
-        split_axis=1,
-        concat_axis=1,
-        tiled=True,
-    )
+    panel = send_rows.reshape(local_feats, peers, grad_cap)
+    latest = lax.axis_size("dp")
+    opened = jnp.split(panel, latest, axis=1)
+    response = jnp.stack(opened, axis=0)
+    block_now = lax.all_to_all(response, split_axis=0, axis_name="dp", concat_axis=0)
+    recv_rows = jnp.concatenate(block_now, axis=1)
     landing = selection_matrix(recv_rows.reshape(local_feats, grad_total), rows_per_shard)
     summed = jnp.einsum(
         "wjc,wjl->wcl",

time: 635 us -> 670 us (1.055)
  local copies, waits for them, and re-layouts: 34.7 us -> 71 us
    unnamed x60 -> x159, local copies, waits for them, and re-layouts: 25.1 us -> 60.7 us
    reduce_scatter x4, waiting for transfers between devices: 85.9 us -> 71.5 us  [summed_rounded(): share = lax.psum_scatter(partial, axis, scatter_dimension=0, tiled=True)]
    all_to_all x1, waiting for transfers between devices: 49 us -> 58.5 us  [local(): lax.all_to_all(send_grads.reshape(local_feats, peers, grad_cap, width), '...]
  transfers between devices with their start and end apart: 8 -> 8, of which waited for: 7 -> 7; matrix products, arithmetic and copies ran while one was open for 6% -> 11% of each run, Pallas kernels for 0% -> 0%
where the time goes in v1:
time: 670 us; the launch traced here: 667 us
  blocking collectives  326 us (49%)
  waiting for transfers between devices  187 us (28%)
  local copies, waits for them, and re-layouts  71 us (11%)
  matrix products  32.4 us (5%)
  starting transfers between devices  20.9 us (3%)
  other arithmetic  16.2 us (2%)
  between operations  14.5 us (2%)
    psum x1, blocking collectives, local(): grad_small = lax.psum(jnp.stack(bias_grads + [head_grad]), 'dp')  247 us
    reduce_scatter x4, waiting for transfers between devices, summed_rounded(): share = lax.psum_scatter(partial, axis, scatter_dimension=0, tiled=True)  71.5 us
    unnamed x159, local copies, waits for them, and re-layouts  60.7 us
    all_to_all x1, waiting for transfers between devices, local(): lax.all_to_all(send_grads.reshape(local_feats, peers, grad_cap, width), '...  58.5 us
    all_gather x4, blocking collectives, summed_rounded(): return lax.all_gather(share.astype(jnp.bfloat16), axis, axis=0, tiled=True)  49.2 us
    all_to_all x1, waiting for transfers between devices, local(): lax.all_to_all(served.reshape(local_feats, peers, look_cap, width), 'dp',...  48.8 us
    all_to_all x1, blocking collectives, local(): lax.all_to_all(wanted.reshape(local_feats, peers, look_cap), 'dp', split_...  21.1 us
  transfers between devices with their start and end apart: 8, of which 7 were waited for; matrix products, arithmetic and copies ran while one was open for 11% of the time, Pallas kernels for 0%

profile of v1, /device:TPU:0, one launch (start us, length us, event | category | flops | bytes accessed | tf_op | source)
XLA Modules:
  0.0 667.5 jit_solution(11305859581277381816)
XLA Ops:
  10.6 8.1 %scatter_custom_fusion.1 = s32[4096]{0:T(1024)S(1)} fusion(s32[2048]{0:T(1024)S(1)} %bitcast.246, s32[2048]{0:T(1024)S(1)} %bitcast.248, s32[]{:T(128)} %constant.5.clone.1), kind=kCustom, calls=%fused_computation.169 | custom fusion | bytes 16388
  18.9 21.1 %all_to_all.20 = s32[4,64,16]{2,0,1:T(4,128)S(1)} all-to-all(s32[4,64,16]{2,0,1:T(4,128)S(1)} %copy.205), channel_id=1, replica_groups=mesh['dp'=64,'mp'=4] {'dp'}, dimensions={1} | all-to-all | bytes 32768 | tf_op jit(solution)/shard_map/all_to_all | solution.py:133
  43.8 4.7 all-to-all-start.3
  51.0 48.8 %all-to-all-done.3 = bf16[4,64,16,256]{3,2,0,1:T(8,128)(2,1)S(1)} async-done(((bf16[4,64,16,256]{3,2,0,1:T(8,128)(2,1)}), bf16[4,64,16,256]{3,2,0,1:T(8,128)(2,1)S(1)}, u32[]{:S(2)}, u32[]{:S(2)}) %all-to-all-start.3) | async-done | bytes 2097184 | tf_op jit(solution)/shard_map/all_to_all | solution.py:143
  103.7 20.2 %reduce-scatter.6.cloned.1.call-done = f32[64,512]{1,0:T(8,128)} async-done(((f32[256,512]{1,0:T(8,128)}), f32[64,512]{1,0:T(8,128)}) %reduce-scatter.6.cloned.1.call-update) | async-done | bytes 131088 | tf_op jit(solution)/shard_map/reduce_scatter | solution.py:63
  125.0 12.3 %all_gather.12 = bf16[256,512]{1,0:T(8,128)(2,1)S(1)} all-gather(bf16[64,512]{1,0:T(8,128)(2,1)S(1)} %convert_element_type.138), channel_id=1, replica_groups=mesh['dp'=64,'mp'=4] {'mp'}, dimensions={0}, use_global_device_ids=true | all-gather | bytes 327680 | tf_op jit(solution)/shard_map/all_gather | solution.py:64
  141.5 23.8 %reduce-scatter.8.cloned.1.call-done = f32[64,512]{1,0:T(8,128)} async-done(((f32[256,512]{1,0:T(8,128)}), f32[64,512]{1,0:T(8,128)}) %reduce-scatter.8.cloned.1.call-update) | async-done | bytes 131088 | tf_op jit(solution)/shard_map/reduce_scatter | solution.py:63
  166.2 12.3 %all_gather.13 = bf16[256,512]{1,0:T(8,128)(2,1)S(1)} all-gather(bf16[64,512]{1,0:T(8,128)(2,1)S(1)} %convert_element_type.141), channel_id=1, replica_groups=mesh['dp'=64,'mp'=4] {'mp'}, dimensions={0}, use_global_device_ids=true | all-gather | bytes 327680 | tf_op jit(solution)/shard_map/all_gather | solution.py:64
  178.5 2.9 fusion.23
  181.3 8.4 %psum.14 = f32[256]{0:T(256)S(1)} all-reduce(f32[256]{0:T(256)S(1)} %get-tuple-element.40), channel_id=1, replica_groups=mesh['dp'=64,'mp'=4] {'mp'}, use_global_device_ids=true, to_apply=%region_8.0 | all-reduce | flops 256 | bytes 2048 | tf_op jit(solution)/shard_map/psum | solution.py:175
  193.4 8.1 %scatter_custom_fusion = s32[4096]{0:T(1024)S(1)} fusion(s32[2048]{0:T(1024)S(1)} %bitcast.247, s32[2048]{0:T(1024)S(1)} %bitcast.249, s32[]{:T(128)} %constant.11.clone.1), kind=kCustom, calls=%fused_computation.171 | custom fusion | bytes 16388
  205.6 11.5 %reduce-scatter.10.cloned.1.call-done = f32[64,512]{1,0:T(8,128)} async-done(((f32[256,512]{1,0:T(8,128)}), f32[64,512]{1,0:T(8,128)}) %reduce-scatter.10.cloned.1.call-update) | async-done | bytes 131088 | tf_op jit(solution)/shard_map/reduce_scatter | solution.py:63
  218.2 12.4 %all_gather.14 = bf16[256,512]{1,0:T(8,128)(2,1)S(1)} all-gather(bf16[64,512]{1,0:T(8,128)(2,1)S(1)} %convert_element_type.149), channel_id=1, replica_groups=mesh['dp'=64,'mp'=4] {'mp'}, dimensions={0}, use_global_device_ids=true | all-gather | bytes 327680 | tf_op jit(solution)/shard_map/all_gather | solution.py:64
  242.9 15.9 %reduce-scatter.12.cloned.1.call-done = f32[64,512]{1,0:T(8,128)} async-done(((f32[256,512]{1,0:T(8,128)}), f32[64,512]{1,0:T(8,128)}) %reduce-scatter.12.cloned.1.call-update) | async-done | bytes 131088 | tf_op jit(solution)/shard_map/reduce_scatter | solution.py:63
  259.9 12.3 %all_gather.15 = bf16[256,512]{1,0:T(8,128)(2,1)S(1)} all-gather(bf16[64,512]{1,0:T(8,128)(2,1)S(1)} %convert_element_type.152), channel_id=1, replica_groups=mesh['dp'=64,'mp'=4] {'mp'}, dimensions={0}, use_global_device_ids=true | all-gather | bytes 327680 | tf_op jit(solution)/shard_map/all_gather | solution.py:64
  272.6 5.3 pad_maximum_fusion
  309.4 10.4 %all-to-all-start = ((s32[64,4,1,16]{3,2,1,0:T(1,128)}), s32[64,4,1,16]{3,2,1,0:T(1,128)S(1)}, u32[]{:S(2)}, u32[]{:S(2)}) async-start(s32[64,4,1,16]{3,2,1,0:T(1,128)} %bitcast.65), calls=%async_computation | async-start | bytes 262144 | tf_op jit(solution)/shard_map/all_to_all | solution.py:113
  323.0 7.8 %all-to-all-done = s32[64,4,1,16]{3,2,1,0:T(1,128)S(1)} async-done(((s32[64,4,1,16]{3,2,1,0:T(1,128)}), s32[64,4,1,16]{3,2,1,0:T(1,128)S(1)}, u32[]{:S(2)}, u32[]{:S(2)}) %all-to-all-start) | async-done | bytes 16416 | tf_op jit(solution)/shard_map/all_to_all | solution.py:113
  330.8 5.6 all-to-all-start.1
  336.4 2.9 copy.200
  339.5 58.5 %all-to-all-done.1 = bf16[4,64,16,256]{3,2,0,1:T(8,128)(2,1)} async-done(((bf16[4,64,16,256]{3,2,0,1:T(8,128)(2,1)}), bf16[4,64,16,256]{3,2,0,1:T(8,128)(2,1)}, u32[]{:S(2)}, u32[]{:S(2)}) %all-to-all-start.1) | async-done | bytes 2097184 | tf_op jit(solution)/shard_map/all_to_all | solution.py:102
  399.8 2.9 multiply_reduce_fusion
  405.2 3.0 copy.211
  409.5 247.1 %psum.15 = f32[3,1024]{1,0:T(4,128)} all-reduce(f32[3,1024]{1,0:T(4,128)S(1)} %pad_maximum_fusion.1), channel_id=1, replica_groups=mesh['dp'=64,'mp'=4] {'dp'}, use_global_device_ids=true, to_apply=%region_15.0 | all-reduce | flops 3072 | bytes 24576 | tf_op jit(solution)/shard_map/psum | solution.py:199
  (227 shorter events, 86.8 us)
Async XLA Ops:
  7.2 312.7 %copy-start = (bf16[4,512,256]{2,1,0:T(8,128)(2,1)S(1)}, bf16[4,512,256]{2,1,0:T(8,128)(2,1)}, u32[]{:S(2)}) copy-start(bf16[4,512,256]{2,1,0:T(8,128)(2,1)} %param.15) | copy-start | bytes 3145732
  7.2 32.8 %copy-start.9 = (f32[4,512,256]{2,1,0:T(8,128)S(1)}, f32[4,512,256]{2,1,0:T(8,128)}, u32[]{:S(2)}) copy-start(f32[4,512,256]{2,1,0:T(8,128)} %param.13) | copy-start | bytes 6291460
  43.8 56.1 %all-to-all-start.3 = ((bf16[4,64,16,256]{3,2,0,1:T(8,128)(2,1)}), bf16[4,64,16,256]{3,2,0,1:T(8,128)(2,1)S(1)}, u32[]{:S(2)}, u32[]{:S(2)}) async-start(bf16[4,64,16,256]{3,2,0,1:T(8,128)(2,1)} %copy.207), calls=%async_computation.3 | async-start | bytes 4194304 | tf_op jit(solution)/shard_map/all_to_all | solution.py:143
  48.5 75.4 %reduce-scatter.6.cloned.1.call-start = ((), (), s32[]{:S(2)}) async-start(), calls=%async_computation.9 | async-start | bytes 655360 | tf_op jit(solution)/shard_map/reduce_scatter | solution.py:63
  103.4 61.9 %reduce-scatter.8.cloned.1.call-start = ((), (), s32[]{:S(2)}) async-start(), calls=%async_computation.10 | async-start | bytes 655360 | tf_op jit(solution)/shard_map/reduce_scatter | solution.py:63
  123.9 16.2 %copy-start.13 = (bf16[2,512,1024]{2,1,0:T(8,128)(2,1)S(1)}, bf16[2,512,1024]{2,1,0:T(8,128)(2,1)}, u32[]{:S(2)}) copy-start(bf16[2,512,1024]{2,1,0:T(8,128)(2,1)} %param.23) | copy-start | bytes 6291460
  140.1 41.2 %copy-start.4 = (bf16[256,1024]{1,0:T(8,128)(2,1)}, bf16[256,1024]{1,0:T(8,128)(2,1)S(1)}, u32[]{:S(2)}) copy-start(bf16[256,1024]{1,0:T(8,128)(2,1)S(1)} %get-tuple-element.124) | copy-start | bytes 1572868
  141.4 75.7 %reduce-scatter.10.cloned.1.call-start = ((), (), s32[]{:S(2)}) async-start(), calls=%async_computation.11 | async-start | bytes 655360 | tf_op jit(solution)/shard_map/reduce_scatter | solution.py:63
  166.2 23.6 %copy-start.39 = (s32[256]{0:T(256)S(1)}, s32[256]{0:T(256)}, u32[]{:S(2)}) copy-start(s32[256]{0:T(256)} %param.21) | copy-start | bytes 3076
  181.3 12.0 %copy-start.35 = (s32[4,512]{1,0:T(4,128)S(1)}, s32[4,512]{1,0:T(4,128)}, u32[]{:S(2)}) copy-start(s32[4,512]{1,0:T(4,128)} %param.17) | copy-start | bytes 24580
  193.3 65.5 %reduce-scatter.12.cloned.1.call-start = ((), (), s32[]{:S(2)}) async-start(), calls=%async_computation.12 | async-start | bytes 655360 | tf_op jit(solution)/shard_map/reduce_scatter | solution.py:63
  217.1 16.5 %copy-start.3 = (bf16[2,512,1024]{2,1,0:T(8,128)(2,1)S(1)}, bf16[2,512,1024]{2,1,0:T(8,128)(2,1)}, u32[]{:S(2)}) copy-start(bf16[2,512,1024]{2,1,0:T(8,128)(2,1)} %param.22) | copy-start | bytes 6291460
  234.9 424.5 %reduce-scatter.14.cloned.1.call-start = ((), (), s32[]{:S(2)}) async-start(), calls=%async_computation.13 | async-start | bytes 8519680 | tf_op jit(solution)/shard_map/reduce_scatter | solution.py:33
  258.8 13.8 %copy-start.2 = (f32[1,512,1024]{2,1,0:T(8,128)S(1)}, f32[1,512,1024]{2,1,0:T(8,128)}, u32[]{:S(2)}) copy-start(f32[1,512,1024]{2,1,0:T(8,128)} %convolution_bitcast_fusion.2) | copy-start | bytes 6291460
  278.0 5.7 copy-start.23
  278.0 6.3 copy-start.22
  278.0 6.9 %copy-start.21 = (s32[4,1,16]{2,1,0:T(1,128)S(1)}, s32[4,1,16]{2,1,0:T(1,128)}, u32[]{:S(2)}) copy-start(s32[4,1,16]{2,1,0:T(1,128)} %get-tuple-element.94) | copy-start | bytes 772
  278.0 7.4 %copy-start.20 = (s32[4,1,16]{2,1,0:T(1,128)S(1)}, s32[4,1,16]{2,1,0:T(1,128)}, u32[]{:S(2)}) copy-start(s32[4,1,16]{2,1,0:T(1,128)} %get-tuple-element.93) | copy-start | bytes 772
  278.0 8.0 %copy-start.19 = (s32[4,1,16]{2,1,0:T(1,128)S(1)}, s32[4,1,16]{2,1,0:T(1,128)}, u32[]{:S(2)}) copy-start(s32[4,1,16]{2,1,0:T(1,128)} %get-tuple-element.92) | copy-start | bytes 772
  278.0 8.5 %copy-start.18 = (s32[4,1,16]{2,1,0:T(1,128)S(1)}, s32[4,1,16]{2,1,0:T(1,128)}, u32[]{:S(2)}) copy-start(s32[4,1,16]{2,1,0:T(1,128)} %get-tuple-element.91) | copy-start | bytes 772
  278.1 9.1 %copy-start.17 = (s32[4,1,16]{2,1,0:T(1,128)S(1)}, s32[4,1,16]{2,1,0:T(1,128)}, u32[]{:S(2)}) copy-start(s32[4,1,16]{2,1,0:T(1,128)} %get-tuple-element.90) | copy-start | bytes 772
  309.4 21.5 %all-to-all-start = ((s32[64,4,1,16]{3,2,1,0:T(1,128)}), s32[64,4,1,16]{3,2,1,0:T(1,128)S(1)}, u32[]{:S(2)}, u32[]{:S(2)}) async-start(s32[64,4,1,16]{3,2,1,0:T(1,128)} %bitcast.65), calls=%async_computation | async-start | bytes 262144 | tf_op jit(solution)/shard_map/all_to_all | solution.py:113
  330.8 67.2 %all-to-all-start.1 = ((bf16[4,64,16,256]{3,2,0,1:T(8,128)(2,1)}), bf16[4,64,16,256]{3,2,0,1:T(8,128)(2,1)}, u32[]{:S(2)}, u32[]{:S(2)}) async-start(bf16[4,64,16,256]{3,2,0,1:T(8,128)(2,1)} %copy.197), calls=%async_computation.1 | async-start | bytes 4194304 | tf_op jit(solution)/shard_map/all_to_all | solution.py:102
  405.2 251.3 %copy-start.6 = (f32[256,1024]{1,0:T(8,128)S(1)}, f32[256,1024]{1,0:T(8,128)}, u32[]{:S(2)}) copy-start(f32[256,1024]{1,0:T(8,128)} %get-tuple-element.126) | copy-start | bytes 3145732
  (26 other events, 75.3 us)
Sparse Core Ops, SparseCore 0:
  103.5 20.3 reduce-scatter.5
  141.5 23.7 reduce-scatter.7
  193.4 23.5 reduce-scatter.9
  235.0 23.7 reduce-scatter.11
  278.2 166.7 reduce-scatter.13
